TPU v7x, 32 devices: a whole 2x2x4 slice. The times are simulated.
32 devices in a mesh: brick: 4 (over z), batch: 8 (over y, x, core).
Axes of the slice: x: 2, y: 2, z: 4, core: 2. Of those that a mesh axis runs over, the one named last changes fastest.
Arguments:
- coarse: bfloat16 [8, 4, 4, 8, 1024], P('batch', 'brick'), may hold values from -6 to 6
- coarse_mask: int32 [8, 4, 256], P('batch', 'brick'), may hold values 0 or 1
- skip: bfloat16 [8, 4, 8, 16, 1024], P('batch', 'brick'), may hold values from -6 to 6
- fine_mask: int32 [8, 4, 2048], P('batch', 'brick'), may hold values 0 or 1
- up_weight: bfloat16 [27, 64, 128], replicated, may hold values from -0.25 to 0.25
- fine_grad: bfloat16 [8, 4, 8, 16, 1024], P('batch', 'brick'), may hold values from -6 to 6
Outputs:
- fine_out: bfloat16 [8, 4, 8, 16, 1024], P('batch', 'brick')
- coarse_grad: bfloat16 [8, 4, 4, 8, 1024], P('batch', 'brick')
- weight_grad: float32 [27, 64, 128], replicated
All inputs are finite; a program needn't handle non-finite values. No bound on the sum of `coarse_mask` or of `fine_mask` on one device may be relied on, other than what follows from the above.
Results may differ from a plain program's by a relative error of at most 0.0035.
Values may be sent and summed in bfloat16 or wider, within the bound.
No kernel may reach another device: no remote copies, remote signals or barrier semaphores. Data moves between devices by JAX's collectives and lax.ppermute only.
A program may use at most 64 MiB of HBM per device.

v0:
```python
import math
import jax
import jax.numpy as jnp
from jax import lax
from jax.sharding import PartitionSpec as P

EVEN_TAPS = ((1, 0),)
ODD_TAPS = ((2, 0), (0, 1))
DIRECTIONS = ((1, 0, 0), (0, 1, 0), (0, 0, 1), (1, 1, 0), (1, 0, 1), (0, 1, 1), (1, 1, 1))
STRIDES = (4, 2, 1)


def from_behind(shard, axis, by):
    size = lax.axis_size(axis)
    pairs = [(i, i + by) for i in range(size) if 0 <= i + by < size]
    return lax.ppermute(shard, axis, pairs)


def tap_pairs(parity):
    if parity == 0:
        return EVEN_TAPS
    return ODD_TAPS


def spread(padded, weight):
    counts = (padded.shape[0] - 1, padded.shape[1] - 1, padded.shape[2] - 1)
    outputs = weight.shape[1]
    parts = []
    for parity_x in range(2):
        for parity_y in range(2):
            for parity_z in range(2):
                total = jnp.zeros(counts + (outputs,), jnp.float32)
                for tap_x, start_x in tap_pairs(parity_x):
                    for tap_y, start_y in tap_pairs(parity_y):
                        for tap_z, start_z in tap_pairs(parity_z):
                            window = padded[
                                start_x : start_x + counts[0],
                                start_y : start_y + counts[1],
                                start_z : start_z + counts[2],
                            ]
                            total = total + jnp.einsum(
                                "abci,oi->abco",
                                window,
                                weight[9 * tap_x + 3 * tap_y + tap_z],
                                preferred_element_type=jnp.float32,
                            )
                parts.append(total)
    stacked = jnp.stack(parts).reshape((2, 2, 2) + counts + (outputs,))
    return stacked.transpose(3, 0, 4, 1, 5, 2, 6).reshape(
        2 * counts[0], 2 * counts[1], 2 * counts[2], outputs
    )


def pick(field, tap, count, axis):
    return lax.slice_in_dim(field, tap, tap + 2 * count - 1, 2, axis)


def adjoint(widened, masked, weight):
    counts = masked.shape[:3]
    back = jnp.zeros(masked.shape, jnp.float32)
    grads = []
    for tap_x in range(3):
        along_x = pick(widened, tap_x, counts[0], 0)
        for tap_y in range(3):
            along_y = pick(along_x, tap_y, counts[1], 1)
            for tap_z in range(3):
                chosen = pick(along_y, tap_z, counts[2], 2)
                index = 9 * tap_x + 3 * tap_y + tap_z
                back = back + jnp.einsum(
                    "abco,oi->abci", chosen, weight[index], preferred_element_type=jnp.float32
                )
                grads.append(
                    jnp.einsum("abco,abci->oi", chosen, masked, preferred_element_type=jnp.float32)
                )
    return (back, jnp.stack(grads))


def offset(direction):
    return 4 * direction[0] + 2 * direction[1] + direction[2]


def allowed(direction, grid_y, grid_z, side):
    result = grid_y >= 0
    if direction[1]:
        result = result & (grid_y == side)
    if direction[2]:
        result = result & (grid_z == side)
    return result


def flatten(piece):
    return piece.reshape(piece.shape[0], -1)


def segment_index(other, axis, edge):
    if other < axis:
        return slice(1, None)
    if other > axis:
        return slice(None)
    return edge


def unit_of(axis):
    return tuple((1 if other == axis else 0 for other in range(3)))


def body(coarse, coarse_mask, skip, fine_mask, up_weight, fine_grad):
    rank = lax.axis_index("brick")
    grid_y = rank // 2 % 2
    grid_z = rank % 2
    size_x, size_y, merged = coarse.shape[2:]
    channels_out = up_weight.shape[1]
    channels_in = up_weight.shape[2]
    size_z = merged // channels_in
    fine_x, fine_y, fine_merged = skip.shape[2:]
    fine_z = fine_merged // channels_out
    coarse_keep = coarse_mask.reshape(size_x, size_y, size_z, 1).astype(jnp.bfloat16)
    masked = coarse.reshape(size_x, size_y, size_z, channels_in) * coarse_keep
    extended = spread(jnp.pad(masked, ((1, 1), (1, 1), (1, 1), (0, 0))), up_weight)[1:, 1:, 1:]
    for axis in range(3):
        source = tuple((segment_index(other, axis, slice(0, 1)) for other in range(3)))
        piece = extended[source]
        got = from_behind(flatten(piece).astype(jnp.bfloat16), "brick", -STRIDES[axis]).astype(
            jnp.float32
        )
        got = jnp.where(allowed(unit_of(axis), grid_y, grid_z, 0), got, 0.0).reshape(piece.shape)
        target = tuple((segment_index(other, axis, slice(-1, None)) for other in range(3)))
        extended = extended.at[target].add(got)
    up = extended[1:, 1:, 1:]
    fine_keep = fine_mask.reshape(fine_x, fine_y, fine_z, 1)
    fine = fine_keep.astype(jnp.float32) * (
        skip.reshape(fine_x, fine_y, fine_z, channels_out).astype(jnp.float32) + up
    )
    fine_out = fine.astype(jnp.bfloat16).reshape(skip.shape)
    cotangent = fine_grad.reshape(fine_x, fine_y, fine_z, channels_out) * fine_keep.astype(
        jnp.bfloat16
    )
    widened = jnp.pad(cotangent, ((1, 0), (1, 0), (1, 0), (0, 0)))
    for direction in DIRECTIONS:
        source = tuple((slice(-1, None) if flag else slice(None) for flag in direction))
        piece = cotangent[source]
        got = from_behind(flatten(piece), "brick", offset(direction))
        got = jnp.where(allowed(direction, grid_y, grid_z, 1), got, 0.0).reshape(piece.shape)
        target = tuple((slice(0, 1) if flag else slice(1, None) for flag in direction))
        widened = widened.at[target].set(got)
    back, grads = adjoint(widened, masked, up_weight)
    coarse_grad = (
        (back * coarse_keep.astype(jnp.float32)).astype(jnp.bfloat16).reshape(coarse.shape)
    )
    summed = lax.psum(grads, ("brick", "batch"))
    scale = 1.0 / math.sqrt(
        lax.axis_size("brick") * lax.axis_size("batch") * size_x * size_y * size_z
    )
    return (fine_out, coarse_grad, summed * scale)


def solution(mesh):
    in_specs = (
        P("batch", "brick", None, None, None),
        P("batch", "brick", None),
        P("batch", "brick", None, None, None),
        P("batch", "brick", None),
        P(),
        P("batch", "brick", None, None, None),
    )
    out_specs = (P("batch", "brick", None, None, None), P("batch", "brick", None, None, None), P())
    return jax.shard_map(body, mesh=mesh, in_specs=in_specs, out_specs=out_specs, check_vma=False)
```

profile of v0, /device:TPU:0, one launch (start us, length us, event | category | flops | bytes accessed | tf_op | source)
XLA Modules:
  0.0 260.1 jit_solution(2375744965565836065)
XLA Ops:
  7.2 1.4 reshape.523
  11.3 5.9 %collective-permute-start.4 = (bf16[8,1024]{1,0:T(8,128)(2,1)S(1)}, bf16[8,1024]{1,0:T(8,128)(2,1)S(1)}, u32[]{:S(2)}, u32[]{:S(2)}) collective-permute-start(bf16[8,1024]{1,0:T(8,128)(2,1)S(1)} %reshape.526), channel_id=1, source_target_pairs={{0,16},{8,24},{1,17},{9,25},{2,18},{10,26},{3,19},{11,27},{4,20},{... | collective-permute-start | bytes 49160 | tf_op jit(solution)/shard_map/ppermute | solution.py:16
  17.6 3.5 %collective-permute-start.5 = (bf16[8,1024]{1,0:T(8,128)(2,1)S(1)}, bf16[8,1024]{1,0:T(8,128)(2,1)S(1)}, u32[]{:S(2)}, u32[]{:S(2)}) collective-permute-start(bf16[8,1024]{1,0:T(8,128)(2,1)S(1)} %reshape.528), channel_id=1, source_target_pairs={{0,8},{8,16},{16,24},{1,9},{9,17},{17,25},{2,10},{10,18},{18,26},{... | collective-permute-start | bytes 49160 | tf_op jit(solution)/shard_map/ppermute | solution.py:16
  31.6 2.0 copy.82
  33.7 2.4 reshape.518
  36.1 1.5 slice.770
  37.6 1.3 pad.47
  39.8 2.2 reshape.539
  42.7 1.3 collective-permute-start.8
  44.0 1.3 collective-permute-done.8
  46.0 1.3 collective-permute-start
  48.5 1.4 scatter.26
  50.5 1.1 fusion.189
  51.6 1.3 slice.733
  53.0 1.3 slice.734
  54.2 1.3 slice.735
  55.5 1.3 slice.737
  56.8 1.3 slice.738
  58.1 1.3 slice.739
  59.4 1.3 slice.741
  60.6 1.3 slice.742
  61.9 1.3 slice.743
  63.2 2.4 fusion.190
  65.6 2.8 %slice.746 = bf16[4,8,8,64]{3,2,1,0:T(8,128)(2,1)} slice(bf16[4,8,17,64]{3,2,1,0:T(8,128)(2,1)} %get-tuple-element.135), slice={[0:4:1], [0:8:1], [0:15:2], [0:64:1]} | slice | bytes 65536 | tf_op jit(solution)/shard_map/slice | solution.py:55
  68.4 2.8 %slice.747 = bf16[4,8,8,64]{3,2,1,0:T(8,128)(2,1)} slice(bf16[4,8,17,64]{3,2,1,0:T(8,128)(2,1)} %get-tuple-element.135), slice={[0:4:1], [0:8:1], [1:16:2], [0:64:1]} | slice | bytes 65536 | tf_op jit(solution)/shard_map/slice | solution.py:55
  71.1 2.8 %slice.748 = bf16[4,8,8,64]{3,2,1,0:T(8,128)(2,1)} slice(bf16[4,8,17,64]{3,2,1,0:T(8,128)(2,1)} %get-tuple-element.135), slice={[0:4:1], [0:8:1], [2:17:2], [0:64:1]} | slice | bytes 65536 | tf_op jit(solution)/shard_map/slice | solution.py:55
  74.0 2.8 %slice.750 = bf16[4,8,8,64]{3,2,1,0:T(8,128)(2,1)} slice(bf16[4,8,17,64]{3,2,1,0:T(8,128)(2,1)} %get-tuple-element.136), slice={[0:4:1], [0:8:1], [0:15:2], [0:64:1]} | slice | bytes 65536 | tf_op jit(solution)/shard_map/slice | solution.py:55
  76.7 2.7 %slice.751 = bf16[4,8,8,64]{3,2,1,0:T(8,128)(2,1)} slice(bf16[4,8,17,64]{3,2,1,0:T(8,128)(2,1)} %get-tuple-element.136), slice={[0:4:1], [0:8:1], [1:16:2], [0:64:1]} | slice | bytes 65536 | tf_op jit(solution)/shard_map/slice | solution.py:55
  79.5 2.8 %slice.752 = bf16[4,8,8,64]{3,2,1,0:T(8,128)(2,1)} slice(bf16[4,8,17,64]{3,2,1,0:T(8,128)(2,1)} %get-tuple-element.136), slice={[0:4:1], [0:8:1], [2:17:2], [0:64:1]} | slice | bytes 65536 | tf_op jit(solution)/shard_map/slice | solution.py:55
  82.3 1.3 slice.754
  83.6 1.3 slice.755
  84.9 1.3 slice.756
  86.1 1.3 slice.759
  87.4 1.3 slice.760
  88.7 1.3 slice.761
  91.1 1.7 fusion.43
  92.9 1.0 fusion.110
  93.9 1.7 fusion.42
  95.6 1.7 fusion.41
  97.3 1.7 fusion.40
  98.9 1.7 fusion.39
  104.7 1.7 fusion.33
  106.4 1.7 fusion.32
  120.4 1.0 convolution_add_fusion.44
  121.4 1.0 convolution_add_fusion.43
  122.5 1.0 convolution_add_fusion.42
  123.5 1.0 convolution_add_fusion.41
  126.9 1.0 convolution_add_fusion.35
  127.9 1.0 convolution_add_fusion.34
  136.7 1.5 convolution_add_fusion.21
  138.3 1.7 fusion.48
  142.7 1.3 collective-permute-start.1
  144.0 1.1 convolution_add_fusion.20
  145.1 4.1 %collective-permute-done.1 = bf16[8,1088]{1,0:T(8,128)(2,1)S(1)} collective-permute-done((bf16[8,1088]{1,0:T(8,128)(2,1)S(1)}, bf16[8,1088]{1,0:T(8,128)(2,1)S(1)}, u32[]{:S(2)}, u32[]{:S(2)}) %collective-permute-start.1) | collective-permute-done | bytes 17440 | tf_op jit(solution)/shard_map/ppermute | solution.py:16
  149.3 1.6 fusion.47
  150.9 1.2 fusion.50
  152.2 1.3 collective-permute-start.2
  155.1 2.8 %collective-permute-done.2 = bf16[8,1024]{1,0:T(8,128)(2,1)S(1)} collective-permute-done((bf16[8,1024]{1,0:T(8,128)(2,1)S(1)}, bf16[8,1024]{1,0:T(8,128)(2,1)S(1)}, u32[]{:S(2)}, u32[]{:S(2)}) %collective-permute-start.2) | collective-permute-done | bytes 16416 | tf_op jit(solution)/shard_map/ppermute | solution.py:16
  158.0 1.1 slice_add_fusion.3
  159.1 3.0 %scatter-add.14 = f32[9,17,17,64]{3,2,1,0:T(8,128)} dynamic-update-slice(f32[9,17,17,64]{3,2,1,0:T(8,128)} %fusion.47, f32[8,16,1,64]{3,2,1,0:T(1,128)S(1)} %slice_add_fusion.3, s32[]{:T(128)} %constant.355.clone.1, s32[]{:T(128)} %constant.355.clone.1, s32[]{:T(128)} %constant.361.clone.1, s32[]{:T(128)} %constant.356.clone.1) | dynamic-update-slice | bytes 65540 | tf_op jit(solution)/shard_map/scatter-add | solution.py:128
  162.1 1.7 fusion.45
  163.8 1.1 reshape.522
  164.9 86.2 %all-reduce.4.cloned.1.call-done = f32[27,64,128]{2,1,0:T(8,128)} async-done(((f32[27,64,128]{2,1,0:T(8,128)}), f32[27,64,128]{2,1,0:T(8,128)}) %all-reduce.4.cloned.1.call-update) | async-done | bytes 884752 | tf_op jit(solution)/shard_map/psum | solution.py:150
  251.1 2.2 broadcast_multiply_fusion
  (208 shorter events, 49.5 us)
Async XLA Ops:
  7.2 18.2 %copy-start.2 = (bf16[27,64,128]{2,1,0:T(8,128)(2,1)S(1)}, bf16[27,64,128]{2,1,0:T(8,128)(2,1)}, u32[]{:S(2)}) copy-start(bf16[27,64,128]{2,1,0:T(8,128)(2,1)} %param.30) | copy-start | bytes 1327108
  7.2 243.9 %all-reduce.4.cloned.1.call-start = ((), (), s32[]{:S(2)}) async-start(), calls=%async_computation | async-start | bytes 1769472 | tf_op jit(solution)/shard_map/psum | solution.py:150
  9.8 17.7 %copy-start.1 = (bf16[8,16,16,64]{3,2,1,0:T(8,128)(2,1)}, bf16[8,16,16,64]{3,2,1,0:T(8,128)(2,1)S(1)}, u32[]{:S(2)}) copy-start(bf16[8,16,16,64]{3,2,1,0:T(8,128)(2,1)S(1)} %broadcast_multiply_fusion.1) | copy-start | bytes 786436
  10.6 37.2 %collective-permute-start.3 = (bf16[1,16384]{1,0:T(2,128)(2,1)}, bf16[1,16384]{1,0:T(2,128)(2,1)S(1)}, u32[]{:S(2)}, u32[]{:S(2)}) collective-permute-start(bf16[1,16384]{1,0:T(2,128)(2,1)} %reshape.524), channel_id=1, source_target_pairs={} | collective-permute-start | bytes 98312 | tf_op jit(solution)/shard_map/ppermute | solution.py:16
  11.3 36.1 %collective-permute-start.4 = (bf16[8,1024]{1,0:T(8,128)(2,1)S(1)}, bf16[8,1024]{1,0:T(8,128)(2,1)S(1)}, u32[]{:S(2)}, u32[]{:S(2)}) collective-permute-start(bf16[8,1024]{1,0:T(8,128)(2,1)S(1)} %reshape.526), channel_id=1, source_target_pairs={{0,16},{8,24},{1,17},{9,25},{2,18},{10,26},{3,19},{11,27},{4,20},{... | collective-permute-start | bytes 49160 | tf_op jit(solution)/shard_map/ppermute | solution.py:16
  17.6 29.9 %collective-permute-start.5 = (bf16[8,1024]{1,0:T(8,128)(2,1)S(1)}, bf16[8,1024]{1,0:T(8,128)(2,1)S(1)}, u32[]{:S(2)}, u32[]{:S(2)}) collective-permute-start(bf16[8,1024]{1,0:T(8,128)(2,1)S(1)} %reshape.528), channel_id=1, source_target_pairs={{0,8},{8,16},{16,24},{1,9},{9,17},{17,25},{2,10},{10,18},{18,26},{... | collective-permute-start | bytes 49160 | tf_op jit(solution)/shard_map/ppermute | solution.py:16
  21.2 24.8 %collective-permute-start.6 = (bf16[1,1024]{1,0:T(2,128)(2,1)S(1)}, bf16[1,1024]{1,0:T(2,128)(2,1)S(1)}, u32[]{:S(2)}, u32[]{:S(2)}) collective-permute-start(bf16[1,1024]{1,0:T(2,128)(2,1)S(1)} %reshape.530), channel_id=1, source_target_pairs={} | collective-permute-start | bytes 6152 | tf_op jit(solution)/shard_map/ppermute | solution.py:16
  21.9 20.8 %collective-permute-start.9 = (bf16[1,64]{1,0:T(2,128)(2,1)S(1)}, bf16[1,64]{1,0:T(2,128)(2,1)S(1)}, u32[]{:S(2)}, u32[]{:S(2)}) collective-permute-start(bf16[1,64]{1,0:T(2,128)(2,1)S(1)} %slice_bitcast_fusion), channel_id=1, source_target_pairs={} | collective-permute-start | bytes 392 | tf_op jit(solution)/shard_map/ppermute | solution.py:16
  36.1 1.5 copy-start.34
  42.7 2.6 collective-permute-start.8
  45.3 2.0 collective-permute-start.7
  46.0 92.3 %collective-permute-start = (bf16[1,18496]{1,0:T(2,128)(2,1)}, bf16[1,18496]{1,0:T(2,128)(2,1)}, u32[]{:S(2)}, u32[]{:S(2)}) collective-permute-start(bf16[1,18496]{1,0:T(2,128)(2,1)} %convert_element_type.107), channel_id=1, source_target_pairs={} | collective-permute-start | bytes 110984 | tf_op jit(solution)/shard_map/ppermute | solution.py:16
  56.8 36.1 %copy-start.3 = (bf16[27,64,128]{2,1,0:T(8,128)(2,1)S(1)}, bf16[27,64,128]{2,1,0:T(8,128)(2,1)}, u32[]{:S(2)}) copy-start(bf16[27,64,128]{2,1,0:T(8,128)(2,1)} %param.30) | copy-start | bytes 1327108
  90.0 10.6 %copy-start.29 = (bf16[4,8,8,64]{3,2,1,0:T(8,128)(2,1)S(1)}, bf16[4,8,8,64]{3,2,1,0:T(8,128)(2,1)}, u32[]{:S(2)}) copy-start(bf16[4,8,8,64]{3,2,1,0:T(8,128)(2,1)} %slice.739) | copy-start | bytes 98308
  90.2 25.3 %copy-start.7 = (bf16[4,8,8,64]{3,2,1,0:T(8,128)(2,1)}, bf16[4,8,8,64]{3,2,1,0:T(8,128)(2,1)S(1)}, u32[]{:S(2)}) copy-start(bf16[4,8,8,64]{3,2,1,0:T(8,128)(2,1)S(1)} %slice.763) | copy-start | bytes 98308
  90.5 10.9 %copy-start.31 = (bf16[4,8,8,64]{3,2,1,0:T(8,128)(2,1)S(1)}, bf16[4,8,8,64]{3,2,1,0:T(8,128)(2,1)}, u32[]{:S(2)}) copy-start(bf16[4,8,8,64]{3,2,1,0:T(8,128)(2,1)} %slice.741) | copy-start | bytes 98308
  90.9 27.8 %copy-start.6 = (bf16[4,8,8,64]{3,2,1,0:T(8,128)(2,1)}, bf16[4,8,8,64]{3,2,1,0:T(8,128)(2,1)S(1)}, u32[]{:S(2)}) copy-start(bf16[4,8,8,64]{3,2,1,0:T(8,128)(2,1)S(1)} %slice.768) | copy-start | bytes 98308
  91.1 28.4 %copy-start.4 = (bf16[4,8,8,64]{3,2,1,0:T(8,128)(2,1)}, bf16[4,8,8,64]{3,2,1,0:T(8,128)(2,1)S(1)}, u32[]{:S(2)}) copy-start(bf16[4,8,8,64]{3,2,1,0:T(8,128)(2,1)S(1)} %slice.769) | copy-start | bytes 98308
  91.1 11.2 %copy-start.25 = (bf16[4,8,8,64]{3,2,1,0:T(8,128)(2,1)S(1)}, bf16[4,8,8,64]{3,2,1,0:T(8,128)(2,1)}, u32[]{:S(2)}) copy-start(bf16[4,8,8,64]{3,2,1,0:T(8,128)(2,1)} %slice.742) | copy-start | bytes 98308
  91.1 12.0 %copy-start.21 = (bf16[4,8,8,64]{3,2,1,0:T(8,128)(2,1)S(1)}, bf16[4,8,8,64]{3,2,1,0:T(8,128)(2,1)}, u32[]{:S(2)}) copy-start(bf16[4,8,8,64]{3,2,1,0:T(8,128)(2,1)} %slice.743) | copy-start | bytes 98308
  91.1 12.8 %copy-start.33 = (bf16[4,8,8,64]{3,2,1,0:T(8,128)(2,1)S(1)}, bf16[4,8,8,64]{3,2,1,0:T(8,128)(2,1)}, u32[]{:S(2)}) copy-start(bf16[4,8,8,64]{3,2,1,0:T(8,128)(2,1)} %slice.746) | copy-start | bytes 98308
  91.1 16.9 %copy-start.32 = (bf16[4,8,8,64]{3,2,1,0:T(8,128)(2,1)S(1)}, bf16[4,8,8,64]{3,2,1,0:T(8,128)(2,1)}, u32[]{:S(2)}) copy-start(bf16[4,8,8,64]{3,2,1,0:T(8,128)(2,1)} %slice.750) | copy-start | bytes 98308
  92.9 16.0 %copy-start.27 = (bf16[4,8,8,64]{3,2,1,0:T(8,128)(2,1)S(1)}, bf16[4,8,8,64]{3,2,1,0:T(8,128)(2,1)}, u32[]{:S(2)}) copy-start(bf16[4,8,8,64]{3,2,1,0:T(8,128)(2,1)} %slice.751) | copy-start | bytes 98308
  95.6 14.1 %copy-start.23 = (bf16[4,8,8,64]{3,2,1,0:T(8,128)(2,1)S(1)}, bf16[4,8,8,64]{3,2,1,0:T(8,128)(2,1)}, u32[]{:S(2)}) copy-start(bf16[4,8,8,64]{3,2,1,0:T(8,128)(2,1)} %slice.752) | copy-start | bytes 98308
  97.3 13.3 %copy-start.19 = (bf16[4,8,8,64]{3,2,1,0:T(8,128)(2,1)S(1)}, bf16[4,8,8,64]{3,2,1,0:T(8,128)(2,1)}, u32[]{:S(2)}) copy-start(bf16[4,8,8,64]{3,2,1,0:T(8,128)(2,1)} %slice.754) | copy-start | bytes 98308
  98.9 12.4 %copy-start.17 = (bf16[4,8,8,64]{3,2,1,0:T(8,128)(2,1)S(1)}, bf16[4,8,8,64]{3,2,1,0:T(8,128)(2,1)}, u32[]{:S(2)}) copy-start(bf16[4,8,8,64]{3,2,1,0:T(8,128)(2,1)} %slice.755) | copy-start | bytes 98308
  100.6 11.5 %copy-start.15 = (bf16[4,8,8,64]{3,2,1,0:T(8,128)(2,1)S(1)}, bf16[4,8,8,64]{3,2,1,0:T(8,128)(2,1)}, u32[]{:S(2)}) copy-start(bf16[4,8,8,64]{3,2,1,0:T(8,128)(2,1)} %slice.756) | copy-start | bytes 98308
  101.5 11.5 %copy-start.13 = (bf16[4,8,8,64]{3,2,1,0:T(8,128)(2,1)S(1)}, bf16[4,8,8,64]{3,2,1,0:T(8,128)(2,1)}, u32[]{:S(2)}) copy-start(bf16[4,8,8,64]{3,2,1,0:T(8,128)(2,1)} %slice.759) | copy-start | bytes 98308
  102.3 11.5 %copy-start.11 = (bf16[4,8,8,64]{3,2,1,0:T(8,128)(2,1)S(1)}, bf16[4,8,8,64]{3,2,1,0:T(8,128)(2,1)}, u32[]{:S(2)}) copy-start(bf16[4,8,8,64]{3,2,1,0:T(8,128)(2,1)} %slice.760) | copy-start | bytes 98308
  103.1 11.5 %copy-start.9 = (bf16[4,8,8,64]{3,2,1,0:T(8,128)(2,1)S(1)}, bf16[4,8,8,64]{3,2,1,0:T(8,128)(2,1)}, u32[]{:S(2)}) copy-start(bf16[4,8,8,64]{3,2,1,0:T(8,128)(2,1)} %slice.761) | copy-start | bytes 98308
  113.8 10.7 %copy-start.30 = (bf16[4,8,8,64]{3,2,1,0:T(8,128)(2,1)S(1)}, bf16[4,8,8,64]{3,2,1,0:T(8,128)(2,1)}, u32[]{:S(2)}) copy-start(bf16[4,8,8,64]{3,2,1,0:T(8,128)(2,1)} %slice.739) | copy-start | bytes 98308
  115.4 10.2 %copy-start.26 = (bf16[4,8,8,64]{3,2,1,0:T(8,128)(2,1)S(1)}, bf16[4,8,8,64]{3,2,1,0:T(8,128)(2,1)}, u32[]{:S(2)}) copy-start(bf16[4,8,8,64]{3,2,1,0:T(8,128)(2,1)} %slice.742) | copy-start | bytes 98308
  116.2 9.6 %copy-start.22 = (bf16[4,8,8,64]{3,2,1,0:T(8,128)(2,1)S(1)}, bf16[4,8,8,64]{3,2,1,0:T(8,128)(2,1)}, u32[]{:S(2)}) copy-start(bf16[4,8,8,64]{3,2,1,0:T(8,128)(2,1)} %slice.743) | copy-start | bytes 98308
  118.7 11.2 %copy-start.28 = (bf16[4,8,8,64]{3,2,1,0:T(8,128)(2,1)S(1)}, bf16[4,8,8,64]{3,2,1,0:T(8,128)(2,1)}, u32[]{:S(2)}) copy-start(bf16[4,8,8,64]{3,2,1,0:T(8,128)(2,1)} %slice.751) | copy-start | bytes 98308
  119.5 10.6 %copy-start.24 = (bf16[4,8,8,64]{3,2,1,0:T(8,128)(2,1)S(1)}, bf16[4,8,8,64]{3,2,1,0:T(8,128)(2,1)}, u32[]{:S(2)}) copy-start(bf16[4,8,8,64]{3,2,1,0:T(8,128)(2,1)} %slice.752) | copy-start | bytes 98308
  120.3 9.9 %copy-start.20 = (bf16[4,8,8,64]{3,2,1,0:T(8,128)(2,1)S(1)}, bf16[4,8,8,64]{3,2,1,0:T(8,128)(2,1)}, u32[]{:S(2)}) copy-start(bf16[4,8,8,64]{3,2,1,0:T(8,128)(2,1)} %slice.754) | copy-start | bytes 98308
  120.3 10.1 %copy-start.18 = (bf16[4,8,8,64]{3,2,1,0:T(8,128)(2,1)S(1)}, bf16[4,8,8,64]{3,2,1,0:T(8,128)(2,1)}, u32[]{:S(2)}) copy-start(bf16[4,8,8,64]{3,2,1,0:T(8,128)(2,1)} %slice.755) | copy-start | bytes 98308
  120.4 10.2 %copy-start.16 = (bf16[4,8,8,64]{3,2,1,0:T(8,128)(2,1)S(1)}, bf16[4,8,8,64]{3,2,1,0:T(8,128)(2,1)}, u32[]{:S(2)}) copy-start(bf16[4,8,8,64]{3,2,1,0:T(8,128)(2,1)} %slice.756) | copy-start | bytes 98308
  120.4 11.2 %copy-start.14 = (bf16[4,8,8,64]{3,2,1,0:T(8,128)(2,1)S(1)}, bf16[4,8,8,64]{3,2,1,0:T(8,128)(2,1)}, u32[]{:S(2)}) copy-start(bf16[4,8,8,64]{3,2,1,0:T(8,128)(2,1)} %slice.759) | copy-start | bytes 98308
  121.4 11.0 %copy-start.12 = (bf16[4,8,8,64]{3,2,1,0:T(8,128)(2,1)S(1)}, bf16[4,8,8,64]{3,2,1,0:T(8,128)(2,1)}, u32[]{:S(2)}) copy-start(bf16[4,8,8,64]{3,2,1,0:T(8,128)(2,1)} %slice.760) | copy-start | bytes 98308
  122.5 10.8 %copy-start.10 = (bf16[4,8,8,64]{3,2,1,0:T(8,128)(2,1)S(1)}, bf16[4,8,8,64]{3,2,1,0:T(8,128)(2,1)}, u32[]{:S(2)}) copy-start(bf16[4,8,8,64]{3,2,1,0:T(8,128)(2,1)} %slice.761) | copy-start | bytes 98308
  123.5 10.7 %copy-start.8 = (bf16[4,8,8,64]{3,2,1,0:T(8,128)(2,1)S(1)}, bf16[4,8,8,64]{3,2,1,0:T(8,128)(2,1)}, u32[]{:S(2)}) copy-start(bf16[4,8,8,64]{3,2,1,0:T(8,128)(2,1)} %copy-done.7) | copy-start | bytes 98308
  130.1 23.4 %copy-start.5 = (bf16[4,8,8,64]{3,2,1,0:T(8,128)(2,1)S(1)}, bf16[4,8,8,64]{3,2,1,0:T(8,128)(2,1)}, u32[]{:S(2)}) copy-start(bf16[4,8,8,64]{3,2,1,0:T(8,128)(2,1)} %copy-done.4) | copy-start | bytes 98308
  130.6 31.5 %copy-start = (f32[8,16,16,64]{3,2,1,0:T(8,128)S(1)}, f32[8,16,16,64]{3,2,1,0:T(8,128)}, u32[]{:S(2)}) copy-start(f32[8,16,16,64]{3,2,1,0:T(8,128)} %reshape.539) | copy-start | bytes 1572868
  142.7 6.5 %collective-permute-start.1 = (bf16[8,1088]{1,0:T(8,128)(2,1)S(1)}, bf16[8,1088]{1,0:T(8,128)(2,1)S(1)}, u32[]{:S(2)}, u32[]{:S(2)}) collective-permute-start(bf16[8,1088]{1,0:T(8,128)(2,1)S(1)} %convert_element_type.109), channel_id=1, source_target_pairs={{16,0},{24,8},{17,1},{25,9},{18,2},{26,10},{19,3},{27,11},{20,4},{... | collective-permute-start | bytes 52232 | tf_op jit(solution)/shard_map/ppermute | solution.py:16
  152.2 5.6 %collective-permute-start.2 = (bf16[8,1024]{1,0:T(8,128)(2,1)S(1)}, bf16[8,1024]{1,0:T(8,128)(2,1)S(1)}, u32[]{:S(2)}, u32[]{:S(2)}) collective-permute-start(bf16[8,1024]{1,0:T(8,128)(2,1)S(1)} %convert_element_type.111), channel_id=1, source_target_pairs={{8,0},{16,8},{24,16},{9,1},{17,9},{25,17},{10,2},{18,10},{26,18},{... | collective-permute-start | bytes 49160 | tf_op jit(solution)/shard_map/ppermute | solution.py:16
Sparse Core Ops, SparseCore 0:
  120.5 130.5 all-reduce.3
where the time goes:
time: 263 us; the launch traced here: 260 us
  waiting for transfers between devices  94.5 us (36%)
  local copies, waits for them, and re-layouts  65.6 us (25%)
  matrix products  55.9 us (21%)
  starting transfers between devices  17.2 us (7%)
  between operations  14.9 us (6%)
  other arithmetic  12.1 us (5%)
    psum x1, waiting for transfers between devices, body(): summed = lax.psum(grads, ('brick', 'batch'))  86.2 us
    slice x30, local copies, waits for them, and re-layouts, pick(): return lax.slice_in_dim(field, tap, tap + 2 * count - 1, 2, axis)  40.5 us
    dot_general x27, matrix products, adjoint(): jnp.einsum('abco,abci->oi', chosen, masked, preferred_element_type=jnp.fl...  28.1 us
    dot_general x27, matrix products, adjoint(): jnp.einsum('abco,oi->abci', chosen, weight[index], preferred_element_type...  20.8 us
    ppermute x10, starting transfers between devices, from_behind(): return lax.ppermute(shard, axis, pairs)  17.2 us
    ppermute x10, waiting for transfers between devices, from_behind(): return lax.ppermute(shard, axis, pairs)  8.22 us
    dot_general x27, matrix products, spread(): jnp.einsum('abci,oi->abco', window, weight[9 * tap_x + 3 * tap_y + tap_z]...  7.06 us
  transfers between devices with their start and end apart: 11, of which 4 were waited for; matrix products, arithmetic and copies ran while one was open for 49% of the time, Pallas kernels for 0%

commit v1 on v0

--- a/solution.py
+++ b/solution.py
@@ -147,7 +147,7 @@
     coarse_grad = (
         (back * coarse_keep.astype(jnp.float32)).astype(jnp.bfloat16).reshape(coarse.shape)
     )
-    summed = lax.psum(grads, ("brick", "batch"))
+    summed = lax.psum(lax.psum(grads, "batch"), "brick")
     scale = 1.0 / math.sqrt(
         lax.axis_size("brick") * lax.axis_size("batch") * size_x * size_y * size_z
     )

time: 263 us -> 243 us (0.924)
  waiting for transfers between devices: 94.5 us -> 69.9 us
    psum x1 -> x2, waiting for transfers between devices: 86.2 us -> 64.9 us  [body(): summed = lax.psum(lax.psum(grads, 'batch'), 'brick')]
    ppermute x10, waiting for transfers between devices: 8.22 us -> 4.93 us  [from_behind(): return lax.ppermute(shard, axis, pairs)]
  transfers between devices with their start and end apart: 11 -> 12, of which waited for: 4 -> 4; matrix products, arithmetic and copies ran while one was open for 49% -> 55% of each run, Pallas kernels for 0% -> 0%
where the time goes in v1:
time: 243 us; the launch traced here: 240 us
  waiting for transfers between devices  69.9 us (29%)
  local copies, waits for them, and re-layouts  67.5 us (28%)
  matrix products  57 us (23%)
  starting transfers between devices  17.8 us (7%)
  between operations  14.8 us (6%)
  other arithmetic  12.7 us (5%)
    psum x2, waiting for transfers between devices, body(): summed = lax.psum(lax.psum(grads, 'batch'), 'brick')  64.9 us
    slice x30, local copies, waits for them, and re-layouts, pick(): return lax.slice_in_dim(field, tap, tap + 2 * count - 1, 2, axis)  40.5 us
    dot_general x27, matrix products, adjoint(): jnp.einsum('abco,abci->oi', chosen, masked, preferred_element_type=jnp.fl...  28.1 us
    dot_general x27, matrix products, adjoint(): jnp.einsum('abco,oi->abci', chosen, weight[index], preferred_element_type...  21.9 us
    ppermute x10, starting transfers between devices, from_behind(): return lax.ppermute(shard, axis, pairs)  17.7 us
    dot_general x27, matrix products, spread(): jnp.einsum('abci,oi->abco', window, weight[9 * tap_x + 3 * tap_y + tap_z]...  7.05 us
    ppermute x10, waiting for transfers between devices, from_behind(): return lax.ppermute(shard, axis, pairs)  4.93 us
  transfers between devices with their start and end apart: 12, of which 4 were waited for; matrix products, arithmetic and copies ran while one was open for 55% of the time, Pallas kernels for 0%

profile of v1, /device:TPU:0, one launch (start us, length us, event | category | flops | bytes accessed | tf_op | source)
XLA Modules:
  0.0 239.7 jit_solution(12851487949499828995)
XLA Ops:
  7.2 1.4 reshape.523
  10.7 5.9 %collective-permute-start.4 = (bf16[8,1024]{1,0:T(8,128)(2,1)S(1)}, bf16[8,1024]{1,0:T(8,128)(2,1)S(1)}, u32[]{:S(2)}, u32[]{:S(2)}) collective-permute-start(bf16[8,1024]{1,0:T(8,128)(2,1)S(1)} %reshape.526), channel_id=1, source_target_pairs={{0,16},{8,24},{1,17},{9,25},{2,18},{10,26},{3,19},{11,27},{4,20},{... | collective-permute-start | bytes 49160 | tf_op jit(solution)/shard_map/ppermute | solution.py:16
  16.9 3.5 %collective-permute-start.5 = (bf16[8,1024]{1,0:T(8,128)(2,1)S(1)}, bf16[8,1024]{1,0:T(8,128)(2,1)S(1)}, u32[]{:S(2)}, u32[]{:S(2)}) collective-permute-start(bf16[8,1024]{1,0:T(8,128)(2,1)S(1)} %reshape.528), channel_id=1, source_target_pairs={{0,8},{8,16},{16,24},{1,9},{9,17},{17,25},{2,10},{10,18},{18,26},{... | collective-permute-start | bytes 49160 | tf_op jit(solution)/shard_map/ppermute | solution.py:16
  21.7 1.2 collective-permute-start.9
  32.6 2.1 copy.82
  34.6 2.4 reshape.518
  37.0 1.5 slice.770
  38.5 1.3 pad.47
  40.7 2.2 reshape.539
  43.7 1.3 collective-permute-start.8
  47.5 1.3 collective-permute-start
  50.7 1.4 scatter.26
  54.4 1.1 fusion.189
  55.5 1.3 slice.733
  56.9 1.3 slice.734
  58.1 1.3 slice.735
  59.4 1.3 slice.737
  60.7 1.3 slice.738
  62.0 1.3 slice.739
  63.3 1.3 slice.741
  64.5 1.3 slice.742
  65.8 1.3 slice.743
  67.1 2.4 fusion.190
  69.5 2.8 %slice.746 = bf16[4,8,8,64]{3,2,1,0:T(8,128)(2,1)} slice(bf16[4,8,17,64]{3,2,1,0:T(8,128)(2,1)} %get-tuple-element.135), slice={[0:4:1], [0:8:1], [0:15:2], [0:64:1]} | slice | bytes 65536 | tf_op jit(solution)/shard_map/slice | solution.py:55
  72.2 2.8 %slice.747 = bf16[4,8,8,64]{3,2,1,0:T(8,128)(2,1)} slice(bf16[4,8,17,64]{3,2,1,0:T(8,128)(2,1)} %get-tuple-element.135), slice={[0:4:1], [0:8:1], [1:16:2], [0:64:1]} | slice | bytes 65536 | tf_op jit(solution)/shard_map/slice | solution.py:55
  75.0 2.8 %slice.748 = bf16[4,8,8,64]{3,2,1,0:T(8,128)(2,1)} slice(bf16[4,8,17,64]{3,2,1,0:T(8,128)(2,1)} %get-tuple-element.135), slice={[0:4:1], [0:8:1], [2:17:2], [0:64:1]} | slice | bytes 65536 | tf_op jit(solution)/shard_map/slice | solution.py:55
  77.8 2.8 %slice.750 = bf16[4,8,8,64]{3,2,1,0:T(8,128)(2,1)} slice(bf16[4,8,17,64]{3,2,1,0:T(8,128)(2,1)} %get-tuple-element.136), slice={[0:4:1], [0:8:1], [0:15:2], [0:64:1]} | slice | bytes 65536 | tf_op jit(solution)/shard_map/slice | solution.py:55
  80.6 2.8 %slice.751 = bf16[4,8,8,64]{3,2,1,0:T(8,128)(2,1)} slice(bf16[4,8,17,64]{3,2,1,0:T(8,128)(2,1)} %get-tuple-element.136), slice={[0:4:1], [0:8:1], [1:16:2], [0:64:1]} | slice | bytes 65536 | tf_op jit(solution)/shard_map/slice | solution.py:55
  83.4 2.8 %slice.752 = bf16[4,8,8,64]{3,2,1,0:T(8,128)(2,1)} slice(bf16[4,8,17,64]{3,2,1,0:T(8,128)(2,1)} %get-tuple-element.136), slice={[0:4:1], [0:8:1], [2:17:2], [0:64:1]} | slice | bytes 65536 | tf_op jit(solution)/shard_map/slice | solution.py:55
  86.2 1.3 slice.754
  87.5 1.3 slice.755
  88.8 1.3 slice.756
  90.1 1.3 slice.759
  91.3 1.3 slice.760
  92.6 1.3 slice.761
  95.0 1.7 fusion.43
  96.8 1.0 fusion.110
  97.8 1.7 fusion.42
  99.5 1.7 fusion.41
  101.1 1.7 fusion.40
  102.8 1.7 fusion.39
  108.6 1.7 fusion.33
  110.3 1.7 fusion.32
  125.3 1.0 convolution_add_fusion.43
  126.3 1.0 convolution_add_fusion.42
  128.3 1.0 convolution_add_fusion.40
  131.4 1.0 convolution_add_fusion.36
  135.4 1.0 convolution_add_fusion.32
  141.6 1.5 convolution_add_fusion.21
  143.1 1.1 fusion.48
  146.1 1.3 collective-permute-start.1
  147.4 1.1 convolution_add_fusion.20
  148.5 4.1 %collective-permute-done.1 = bf16[8,1088]{1,0:T(8,128)(2,1)S(1)} collective-permute-done((bf16[8,1088]{1,0:T(8,128)(2,1)S(1)}, bf16[8,1088]{1,0:T(8,128)(2,1)S(1)}, u32[]{:S(2)}, u32[]{:S(2)}) %collective-permute-start.1) | collective-permute-done | bytes 17440 | tf_op jit(solution)/shard_map/ppermute | solution.py:16
  152.7 1.5 fusion.47
  154.2 1.2 fusion.50
  155.6 1.3 collective-permute-start.2
  156.9 25.4 %all-reduce.5.cloned.1.call-done = f32[27,64,128]{2,1,0:T(8,128)} async-done(((f32[27,64,128]{2,1,0:T(8,128)}), f32[27,64,128]{2,1,0:T(8,128)}) %all-reduce.5.cloned.1.call-update) | async-done | bytes 884752 | tf_op jit(solution)/shard_map/psum | solution.py:150
  182.3 1.0 fusion.16
  184.1 1.1 slice_add_fusion.3
  185.2 2.9 %scatter-add.14 = f32[9,17,17,64]{3,2,1,0:T(8,128)} dynamic-update-slice(f32[9,17,17,64]{3,2,1,0:T(8,128)} %fusion.47, f32[8,16,1,64]{3,2,1,0:T(1,128)S(1)} %slice_add_fusion.3, s32[]{:T(128)} %constant.355.clone.1, s32[]{:T(128)} %constant.355.clone.1, s32[]{:T(128)} %constant.361.clone.1, s32[]{:T(128)} %constant.356.clone.1) | dynamic-update-slice | bytes 65540 | tf_op jit(solution)/shard_map/scatter-add | solution.py:128
  188.2 1.9 fusion.45
  190.1 1.1 reshape.522
  191.1 39.5 %all-reduce.7.cloned.1.call-done = f32[27,64,128]{2,1,0:T(8,128)} async-done(((f32[27,64,128]{2,1,0:T(8,128)}), f32[27,64,128]{2,1,0:T(8,128)}) %all-reduce.7.cloned.1.call-update) | async-done | bytes 884752 | tf_op jit(solution)/shard_map/psum | solution.py:150
  230.6 2.2 broadcast_multiply_fusion
  (197 shorter events, 53.9 us)
Async XLA Ops:
  7.2 19.1 %copy-start.2 = (bf16[27,64,128]{2,1,0:T(8,128)(2,1)S(1)}, bf16[27,64,128]{2,1,0:T(8,128)(2,1)}, u32[]{:S(2)}) copy-start(bf16[27,64,128]{2,1,0:T(8,128)(2,1)} %param.30) | copy-start | bytes 1327108
  7.2 175.1 %all-reduce.5.cloned.1.call-start = ((), (), s32[]{:S(2)}) async-start(), calls=%async_computation | async-start | bytes 1769472 | tf_op jit(solution)/shard_map/psum | solution.py:150
  9.8 18.6 %copy-start.1 = (bf16[8,16,16,64]{3,2,1,0:T(8,128)(2,1)}, bf16[8,16,16,64]{3,2,1,0:T(8,128)(2,1)S(1)}, u32[]{:S(2)}) copy-start(bf16[8,16,16,64]{3,2,1,0:T(8,128)(2,1)S(1)} %broadcast_multiply_fusion.1) | copy-start | bytes 786436
  9.9 40.0 %collective-permute-start.3 = (bf16[1,16384]{1,0:T(2,128)(2,1)S(1)}, bf16[1,16384]{1,0:T(2,128)(2,1)S(1)}, u32[]{:S(2)}, u32[]{:S(2)}) collective-permute-start(bf16[1,16384]{1,0:T(2,128)(2,1)S(1)} %reshape.524), channel_id=1, source_target_pairs={} | collective-permute-start | bytes 98312 | tf_op jit(solution)/shard_map/ppermute | solution.py:16
  10.7 38.9 %collective-permute-start.4 = (bf16[8,1024]{1,0:T(8,128)(2,1)S(1)}, bf16[8,1024]{1,0:T(8,128)(2,1)S(1)}, u32[]{:S(2)}, u32[]{:S(2)}) collective-permute-start(bf16[8,1024]{1,0:T(8,128)(2,1)S(1)} %reshape.526), channel_id=1, source_target_pairs={{0,16},{8,24},{1,17},{9,25},{2,18},{10,26},{3,19},{11,27},{4,20},{... | collective-permute-start | bytes 49160 | tf_op jit(solution)/shard_map/ppermute | solution.py:16
  16.9 32.7 %collective-permute-start.5 = (bf16[8,1024]{1,0:T(8,128)(2,1)S(1)}, bf16[8,1024]{1,0:T(8,128)(2,1)S(1)}, u32[]{:S(2)}, u32[]{:S(2)}) collective-permute-start(bf16[8,1024]{1,0:T(8,128)(2,1)S(1)} %reshape.528), channel_id=1, source_target_pairs={{0,8},{8,16},{16,24},{1,9},{9,17},{17,25},{2,10},{10,18},{18,26},{... | collective-permute-start | bytes 49160 | tf_op jit(solution)/shard_map/ppermute | solution.py:16
  20.5 27.0 %collective-permute-start.6 = (bf16[1,1024]{1,0:T(2,128)(2,1)S(1)}, bf16[1,1024]{1,0:T(2,128)(2,1)S(1)}, u32[]{:S(2)}, u32[]{:S(2)}) collective-permute-start(bf16[1,1024]{1,0:T(2,128)(2,1)S(1)} %reshape.530), channel_id=1, source_target_pairs={} | collective-permute-start | bytes 6152 | tf_op jit(solution)/shard_map/ppermute | solution.py:16
  21.7 22.0 %collective-permute-start.9 = (bf16[1,64]{1,0:T(2,128)(2,1)}, bf16[1,64]{1,0:T(2,128)(2,1)}, u32[]{:S(2)}, u32[]{:S(2)}) collective-permute-start(bf16[1,64]{1,0:T(2,128)(2,1)} %slice_bitcast_fusion), channel_id=1, source_target_pairs={} | collective-permute-start | bytes 392 | tf_op jit(solution)/shard_map/ppermute | solution.py:16
  37.0 1.5 copy-start.27
  43.7 2.6 %collective-permute-start.8 = (bf16[8,64]{1,0:T(8,128)(2,1)S(1)}, bf16[8,64]{1,0:T(8,128)(2,1)S(1)}, u32[]{:S(2)}, u32[]{:S(2)}) collective-permute-start(bf16[8,64]{1,0:T(8,128)(2,1)S(1)} %bitcast.612), channel_id=1, source_target_pairs={{0,24},{1,25},{2,26},{3,27},{4,28},{5,29},{6,30},{7,31}} | collective-permute-start | bytes 3080 | tf_op jit(solution)/shard_map/ppermute | solution.py:16
  46.2 2.6 %collective-permute-start.7 = (bf16[1,1024]{1,0:T(2,128)(2,1)S(1)}, bf16[1,1024]{1,0:T(2,128)(2,1)S(1)}, u32[]{:S(2)}, u32[]{:S(2)}) collective-permute-start(bf16[1,1024]{1,0:T(2,128)(2,1)S(1)} %reshape.532), channel_id=1, source_target_pairs={} | collective-permute-start | bytes 6152 | tf_op jit(solution)/shard_map/ppermute | solution.py:16
  47.5 95.6 %collective-permute-start = (bf16[1,18496]{1,0:T(2,128)(2,1)}, bf16[1,18496]{1,0:T(2,128)(2,1)}, u32[]{:S(2)}, u32[]{:S(2)}) collective-permute-start(bf16[1,18496]{1,0:T(2,128)(2,1)} %convert_element_type.107), channel_id=1, source_target_pairs={} | collective-permute-start | bytes 110984 | tf_op jit(solution)/shard_map/ppermute | solution.py:16
  60.7 36.1 %copy-start.3 = (bf16[27,64,128]{2,1,0:T(8,128)(2,1)S(1)}, bf16[27,64,128]{2,1,0:T(8,128)(2,1)}, u32[]{:S(2)}) copy-start(bf16[27,64,128]{2,1,0:T(8,128)(2,1)} %param.30) | copy-start | bytes 1327108
  93.9 10.6 %copy-start.22 = (bf16[4,8,8,64]{3,2,1,0:T(8,128)(2,1)S(1)}, bf16[4,8,8,64]{3,2,1,0:T(8,128)(2,1)}, u32[]{:S(2)}) copy-start(bf16[4,8,8,64]{3,2,1,0:T(8,128)(2,1)} %slice.739) | copy-start | bytes 98308
  94.4 10.9 %copy-start.23 = (bf16[4,8,8,64]{3,2,1,0:T(8,128)(2,1)S(1)}, bf16[4,8,8,64]{3,2,1,0:T(8,128)(2,1)}, u32[]{:S(2)}) copy-start(bf16[4,8,8,64]{3,2,1,0:T(8,128)(2,1)} %slice.741) | copy-start | bytes 98308
  94.8 27.8 %copy-start.5 = (bf16[4,8,8,64]{3,2,1,0:T(8,128)(2,1)}, bf16[4,8,8,64]{3,2,1,0:T(8,128)(2,1)S(1)}, u32[]{:S(2)}) copy-start(bf16[4,8,8,64]{3,2,1,0:T(8,128)(2,1)S(1)} %slice.768) | copy-start | bytes 98308
  95.0 28.4 %copy-start.4 = (bf16[4,8,8,64]{3,2,1,0:T(8,128)(2,1)}, bf16[4,8,8,64]{3,2,1,0:T(8,128)(2,1)S(1)}, u32[]{:S(2)}) copy-start(bf16[4,8,8,64]{3,2,1,0:T(8,128)(2,1)S(1)} %slice.769) | copy-start | bytes 98308
  95.0 11.2 %copy-start.20 = (bf16[4,8,8,64]{3,2,1,0:T(8,128)(2,1)S(1)}, bf16[4,8,8,64]{3,2,1,0:T(8,128)(2,1)}, u32[]{:S(2)}) copy-start(bf16[4,8,8,64]{3,2,1,0:T(8,128)(2,1)} %slice.742) | copy-start | bytes 98308
  95.0 12.0 %copy-start.16 = (bf16[4,8,8,64]{3,2,1,0:T(8,128)(2,1)S(1)}, bf16[4,8,8,64]{3,2,1,0:T(8,128)(2,1)}, u32[]{:S(2)}) copy-start(bf16[4,8,8,64]{3,2,1,0:T(8,128)(2,1)} %slice.743) | copy-start | bytes 98308
  95.0 12.8 %copy-start.25 = (bf16[4,8,8,64]{3,2,1,0:T(8,128)(2,1)S(1)}, bf16[4,8,8,64]{3,2,1,0:T(8,128)(2,1)}, u32[]{:S(2)}) copy-start(bf16[4,8,8,64]{3,2,1,0:T(8,128)(2,1)} %slice.746) | copy-start | bytes 98308
  95.0 16.9 %copy-start.24 = (bf16[4,8,8,64]{3,2,1,0:T(8,128)(2,1)S(1)}, bf16[4,8,8,64]{3,2,1,0:T(8,128)(2,1)}, u32[]{:S(2)}) copy-start(bf16[4,8,8,64]{3,2,1,0:T(8,128)(2,1)} %slice.750) | copy-start | bytes 98308
  96.8 16.0 %copy-start.21 = (bf16[4,8,8,64]{3,2,1,0:T(8,128)(2,1)S(1)}, bf16[4,8,8,64]{3,2,1,0:T(8,128)(2,1)}, u32[]{:S(2)}) copy-start(bf16[4,8,8,64]{3,2,1,0:T(8,128)(2,1)} %slice.751) | copy-start | bytes 98308
  99.5 14.1 %copy-start.18 = (bf16[4,8,8,64]{3,2,1,0:T(8,128)(2,1)S(1)}, bf16[4,8,8,64]{3,2,1,0:T(8,128)(2,1)}, u32[]{:S(2)}) copy-start(bf16[4,8,8,64]{3,2,1,0:T(8,128)(2,1)} %slice.752) | copy-start | bytes 98308
  101.1 13.3 %copy-start.14 = (bf16[4,8,8,64]{3,2,1,0:T(8,128)(2,1)S(1)}, bf16[4,8,8,64]{3,2,1,0:T(8,128)(2,1)}, u32[]{:S(2)}) copy-start(bf16[4,8,8,64]{3,2,1,0:T(8,128)(2,1)} %slice.754) | copy-start | bytes 98308
  102.8 12.4 %copy-start.12 = (bf16[4,8,8,64]{3,2,1,0:T(8,128)(2,1)S(1)}, bf16[4,8,8,64]{3,2,1,0:T(8,128)(2,1)}, u32[]{:S(2)}) copy-start(bf16[4,8,8,64]{3,2,1,0:T(8,128)(2,1)} %slice.755) | copy-start | bytes 98308
  104.5 11.5 %copy-start.11 = (bf16[4,8,8,64]{3,2,1,0:T(8,128)(2,1)S(1)}, bf16[4,8,8,64]{3,2,1,0:T(8,128)(2,1)}, u32[]{:S(2)}) copy-start(bf16[4,8,8,64]{3,2,1,0:T(8,128)(2,1)} %slice.756) | copy-start | bytes 98308
  105.3 11.5 %copy-start.10 = (bf16[4,8,8,64]{3,2,1,0:T(8,128)(2,1)S(1)}, bf16[4,8,8,64]{3,2,1,0:T(8,128)(2,1)}, u32[]{:S(2)}) copy-start(bf16[4,8,8,64]{3,2,1,0:T(8,128)(2,1)} %slice.759) | copy-start | bytes 98308
  106.2 11.5 %copy-start.8 = (bf16[4,8,8,64]{3,2,1,0:T(8,128)(2,1)S(1)}, bf16[4,8,8,64]{3,2,1,0:T(8,128)(2,1)}, u32[]{:S(2)}) copy-start(bf16[4,8,8,64]{3,2,1,0:T(8,128)(2,1)} %slice.760) | copy-start | bytes 98308
  107.0 11.5 %copy-start.6 = (bf16[4,8,8,64]{3,2,1,0:T(8,128)(2,1)S(1)}, bf16[4,8,8,64]{3,2,1,0:T(8,128)(2,1)}, u32[]{:S(2)}) copy-start(bf16[4,8,8,64]{3,2,1,0:T(8,128)(2,1)} %slice.761) | copy-start | bytes 98308
  120.1 11.2 %copy-start.17 = (bf16[4,8,8,64]{3,2,1,0:T(8,128)(2,1)S(1)}, bf16[4,8,8,64]{3,2,1,0:T(8,128)(2,1)}, u32[]{:S(2)}) copy-start(bf16[4,8,8,64]{3,2,1,0:T(8,128)(2,1)} %slice.743) | copy-start | bytes 98308
  123.4 13.0 %copy-start.19 = (bf16[4,8,8,64]{3,2,1,0:T(8,128)(2,1)S(1)}, bf16[4,8,8,64]{3,2,1,0:T(8,128)(2,1)}, u32[]{:S(2)}) copy-start(bf16[4,8,8,64]{3,2,1,0:T(8,128)(2,1)} %slice.752) | copy-start | bytes 98308
  124.2 12.3 %copy-start.15 = (bf16[4,8,8,64]{3,2,1,0:T(8,128)(2,1)S(1)}, bf16[4,8,8,64]{3,2,1,0:T(8,128)(2,1)}, u32[]{:S(2)}) copy-start(bf16[4,8,8,64]{3,2,1,0:T(8,128)(2,1)} %slice.754) | copy-start | bytes 98308
  124.2 12.5 %copy-start.13 = (bf16[4,8,8,64]{3,2,1,0:T(8,128)(2,1)S(1)}, bf16[4,8,8,64]{3,2,1,0:T(8,128)(2,1)}, u32[]{:S(2)}) copy-start(bf16[4,8,8,64]{3,2,1,0:T(8,128)(2,1)} %slice.755) | copy-start | bytes 98308
  124.2 106.4 %all-reduce.7.cloned.1.call-start = ((), (), s32[]{:S(2)}) async-start(), calls=%async_computation.1 | async-start | bytes 1769472 | tf_op jit(solution)/shard_map/psum | solution.py:150
  125.3 11.9 %copy-start.9 = (bf16[4,8,8,64]{3,2,1,0:T(8,128)(2,1)S(1)}, bf16[4,8,8,64]{3,2,1,0:T(8,128)(2,1)}, u32[]{:S(2)}) copy-start(bf16[4,8,8,64]{3,2,1,0:T(8,128)(2,1)} %slice.760) | copy-start | bytes 98308
  126.3 11.8 %copy-start.7 = (bf16[4,8,8,64]{3,2,1,0:T(8,128)(2,1)S(1)}, bf16[4,8,8,64]{3,2,1,0:T(8,128)(2,1)}, u32[]{:S(2)}) copy-start(bf16[4,8,8,64]{3,2,1,0:T(8,128)(2,1)} %slice.761) | copy-start | bytes 98308
  137.2 51.0 %copy-start = (f32[8,16,16,64]{3,2,1,0:T(8,128)S(1)}, f32[8,16,16,64]{3,2,1,0:T(8,128)}, u32[]{:S(2)}) copy-start(f32[8,16,16,64]{3,2,1,0:T(8,128)} %reshape.539) | copy-start | bytes 1572868
  144.3 43.8 %copy-start.26 = (f32[8,16,16]{2,1,0:T(8,128)S(1)}, f32[8,16,16]{2,1,0:T(8,128)}, u32[]{:S(2)}) copy-start(f32[8,16,16]{2,1,0:T(8,128)} %convert_element_type.102) | copy-start | bytes 24580
  146.1 6.5 %collective-permute-start.1 = (bf16[8,1088]{1,0:T(8,128)(2,1)S(1)}, bf16[8,1088]{1,0:T(8,128)(2,1)S(1)}, u32[]{:S(2)}, u32[]{:S(2)}) collective-permute-start(bf16[8,1088]{1,0:T(8,128)(2,1)S(1)} %convert_element_type.109), channel_id=1, source_target_pairs={{16,0},{24,8},{17,1},{25,9},{18,2},{26,10},{19,3},{27,11},{20,4},{... | collective-permute-start | bytes 52232 | tf_op jit(solution)/shard_map/ppermute | solution.py:16
  155.6 28.4 %collective-permute-start.2 = (bf16[8,1024]{1,0:T(8,128)(2,1)S(1)}, bf16[8,1024]{1,0:T(8,128)(2,1)S(1)}, u32[]{:S(2)}, u32[]{:S(2)}) collective-permute-start(bf16[8,1024]{1,0:T(8,128)(2,1)S(1)} %convert_element_type.111), channel_id=1, source_target_pairs={{8,0},{16,8},{24,16},{9,1},{17,9},{25,17},{10,2},{18,10},{26,18},{... | collective-permute-start | bytes 49160 | tf_op jit(solution)/shard_map/ppermute | solution.py:16
Sparse Core Ops, SparseCore 0:
  124.4 57.8 all-reduce.4
  184.7 45.9 all-reduce.6
